TPU v7x, 512 devices: a whole 4x8x8 slice. The times are simulated.
512 devices in a mesh: rows: 128 (over y_hi, x, z), rep: 4 (over y_lo, core).
Axes of the slice: x: 4, y: 8 (y_hi: 4, y_lo: 2; y = y_hi * 2 + y_lo), z: 8, core: 2. Of those that a mesh axis runs over, the one named last changes fastest.
Arguments:
- features: bfloat16 [65536, 256], P(('rows', 'rep')), may hold values from -6 to 6
- weight: bfloat16 [256, 256], replicated, may hold values from -0.375 to 0.375
- bias_terms: float32 [256], replicated, may hold values from -3 to 3
- tile_data: bfloat16 [128, 4, 8, 128, 128], P('rows'), may hold values from -0.1875 to 0.1875
- tile_row: int32 [128, 4, 8], P('rows'), may hold values from 0 to 3
- tile_col: int32 [128, 4, 8], P('rows'), may hold values from 0 to 127
- tile_count: int32 [128, 4], P('rows'), may hold values from 1 to 8, as said below
- grad_out: bfloat16 [65536, 256], P(('rows', 'rep')), may hold values from -6 to 6
Outputs:
- layer_out: bfloat16 [65536, 256], P(('rows', 'rep'))
- weight_grad: float32 [256, 256], replicated
- bias_grad: float32 [256], replicated
Inputs may be any that keep to these rules, and one draw needn't show every extreme that they name: `tile_count`: some group's stripe has all 8 slots live in every draw.
All inputs are finite; a program needn't handle non-finite values.
Results may differ from a plain program's by a relative error of at most 0.015.
Values may be sent and summed in bfloat16 or wider, within the bound.
No kernel may reach another device: no remote copies, remote signals or barrier semaphores. Data moves between devices by JAX's collectives and lax.ppermute only.
A program may use at most 64 MiB of HBM per device.

v0:
```python
import jax
import jax.numpy as jnp
from jax import lax
from jax.sharding import PartitionSpec as P


def slots_wide(tile_set, row_set, col_set, live_set, blocks, row_count):
    picked = jnp.take(blocks, col_set, axis=0)
    product = jnp.einsum("tij,tjf->tif", tile_set, picked, preferred_element_type=jnp.float32)
    local_ids = jnp.arange(row_count, dtype=jnp.int32)
    select = ((row_set[None, :] == local_ids[:, None]) & live_set[None, :]).astype(jnp.float32)
    return jnp.einsum("bt,tif->bif", select, product)


def propagate(tile_set, row_set, col_set, count_set, blocks, row_count, slot_fn):
    stripes, capacity = row_set.shape
    block_size = tile_set.shape[-1]
    slot_ids = jnp.arange(capacity, dtype=jnp.int32)
    live_set = slot_ids[None, :] < count_set[:, None]
    accumulated = slot_fn(
        tile_set.reshape(-1, block_size, block_size),
        row_set.reshape(-1),
        col_set.reshape(-1),
        live_set.reshape(-1),
        blocks,
        row_count,
    )
    return accumulated


def shards(features, weight, bias_terms, tile_data, tile_row, tile_col, tile_count, grad_out):
    block_size = tile_data.shape[-1]
    feature_width = features.shape[1]
    row_count = lax.axis_size("rep")
    rep_index = lax.axis_index("rep")
    own_tiles = lax.dynamic_slice_in_dim(tile_data[0], rep_index, 1, 0)
    own_rows = lax.dynamic_slice_in_dim(tile_row[0], rep_index, 1, 0)
    own_cols = lax.dynamic_slice_in_dim(tile_col[0], rep_index, 1, 0)
    own_count = lax.dynamic_slice_in_dim(tile_count[0], rep_index, 1, 0)
    stripe_nodes = lax.all_gather(features, "rows", axis=0, tiled=True)
    blocks = stripe_nodes.reshape(-1, block_size, feature_width)
    partial_value = propagate(
        own_tiles, own_rows, own_cols, own_count, blocks, row_count, slots_wide
    )
    partial_value = partial_value.reshape(row_count * block_size, feature_width)
    propagated = lax.psum_scatter(partial_value, "rep", scatter_dimension=0, tiled=True).astype(
        jnp.bfloat16
    )
    preact = jnp.dot(propagated, weight, preferred_element_type=jnp.float32) + bias_terms
    sigma = jax.nn.sigmoid(preact)
    layer_out = (preact * sigma).astype(jnp.bfloat16)
    slope = sigma * (1.0 + preact * (1.0 - sigma))
    grad_pre = (grad_out.astype(jnp.float32) * slope).astype(jnp.bfloat16)
    weight_term = lax.dot_general(
        propagated, grad_pre, (((0,), (0,)), ((), ())), preferred_element_type=jnp.float32
    )
    bias_term = jnp.sum(grad_pre.astype(jnp.float32), axis=0)
    weight_grad, bias_grad = lax.psum((weight_term, bias_term), ("rows", "rep"))
    return (layer_out, weight_grad, bias_grad)


def solution(mesh):
    placed = (
        P(("rows", "rep"), None),
        P(),
        P(),
        P("rows", None, None, None, None),
        P("rows", None, None),
        P("rows", None, None),
        P("rows", None),
        P(("rows", "rep"), None),
    )
    return jax.shard_map(
        shards,
        mesh=mesh,
        in_specs=placed,
        out_specs=(P(("rows", "rep"), None), P(), P()),
        check_vma=False,
    )
```

profile of v0, /device:TPU:23, one launch (start us, length us, event | category | flops | bytes accessed | tf_op | source)
XLA Modules:
  0.0 482.8 jit_solution(15143895187925583589)
XLA Ops:
  7.2 0.0 copy-start
  7.2 0.0 all-gather.2.cloned.1.call-start
  7.2 0.7 all-gather.2.cloned.1.call-update
  7.9 0.0 reduce-scatter.2.cloned.1.call-start
  8.0 1.2 constant_dynamic-slice_fusion.1
  9.2 0.7 fusion.18
  9.9 0.7 compare_and_fusion
  10.6 0.6 iota_compare_fusion.1
  11.2 0.7 fusion.17
  11.9 154.5 %all-gather.2.cloned.1.call-done = bf16[16384,256]{1,0:T(8,128)(2,1)} async-done(((bf16[128,256]{1,0:T(8,128)(2,1)}), bf16[16384,256]{1,0:T(8,128)(2,1)}) %all-gather.2.cloned.1.call-update) | async-done | bytes 8388624 | tf_op jit(solution)/shard_map/all_gather | solution.py:40
  166.5 4.0 gather_fusion
  170.4 0.0 copy-done
  170.4 0.4 fusion.2
  170.8 0.4 fusion
  171.2 0.9 copy.11
  172.1 0.0 reduce-scatter.2.cloned.1.call-update
  172.1 0.0 all-reduce.2.cloned.1.call-start
  172.2 24.1 %reduce-scatter.2.cloned.1.call-done = f32[128,256]{1,0:T(8,128)} async-done(((f32[512,256]{1,0:T(8,128)}), f32[128,256]{1,0:T(8,128)}) %reduce-scatter.2.cloned.1.call-update) | async-done | bytes 131088 | tf_op jit(solution)/shard_map/reduce_scatter | solution.py:46
  196.3 1.8 convert_reduce_fusion
  198.2 1.8 fusion.8
  200.0 0.0 all-reduce.2.cloned.1.call-update
  200.0 96.6 %psum.15 = f32[256]{0:T(256)} all-reduce(f32[256]{0:T(256)S(1)} %get-tuple-element.3), channel_id=1, replica_groups=mesh['rows'=128,'rep'=4] {'rows','rep'}, use_global_device_ids=true, to_apply=%region_3.4 | all-reduce | flops 256 | bytes 2048 | tf_op jit(solution)/shard_map/psum | solution.py:58
  296.6 178.0 %all-reduce.2.cloned.1.call-done = f32[256,256]{1,0:T(8,128)} async-done(((f32[256,256]{1,0:T(8,128)}), f32[256,256]{1,0:T(8,128)}) %all-reduce.2.cloned.1.call-update) | async-done | bytes 262160 | tf_op jit(solution)/shard_map/psum | solution.py:58
  474.6 1.7 copy.16
  (1 shorter events, 0.0 us)
Async XLA Ops:
  7.2 163.3 %copy-start = (bf16[1,4,8,128,128]{4,3,2,1,0:T(8,128)(2,1)S(1)}, bf16[1,4,8,128,128]{4,3,2,1,0:T(8,128)(2,1)}, u32[]{:S(2)}) copy-start(bf16[1,4,8,128,128]{4,3,2,1,0:T(8,128)(2,1)} %param.11) | copy-start | bytes 3145732
  7.2 159.3 %all-gather.2.cloned.1.call-start = ((), (), s32[]{:S(2)}) async-start(), calls=%async_computation.1 | async-start | bytes 8454144 | tf_op jit(solution)/shard_map/all_gather | solution.py:40
  7.9 188.4 %reduce-scatter.2.cloned.1.call-start = ((), (), s32[]{:S(2)}) async-start(), calls=%async_computation.2 | async-start | bytes 655360 | tf_op jit(solution)/shard_map/reduce_scatter | solution.py:46
  172.1 302.5 %all-reduce.2.cloned.1.call-start = ((), (), s32[]{:S(2)}) async-start(), calls=%async_computation.3 | async-start | bytes 524288 | tf_op jit(solution)/shard_map/psum | solution.py:58
Sparse Core Ops, SparseCore 0:
  12.5 153.9 all-gather.1
  172.3 24.0 reduce-scatter.1
  201.9 272.6 all-reduce.1
where the time goes:
time: 483 us
  waiting for transfers between devices  357 us (74%)
  blocking collectives  96.6 us (20%)
  between operations  13.8 us (3%)
  local copies, waits for them, and re-layouts  8.46 us (2%)
    psum x1, waiting for transfers between devices, shards(): weight_grad, bias_grad = lax.psum((weight_term, bias_term), ('rows', 'rep'))  178 us
    all_gather x1, waiting for transfers between devices, shards(): stripe_nodes = lax.all_gather(features, 'rows', axis=0, tiled=True)  155 us
    psum x1, blocking collectives, shards(): weight_grad, bias_grad = lax.psum((weight_term, bias_term), ('rows', 'rep'))  96.6 us
    reduce_scatter x1, waiting for transfers between devices, shards(): lax.psum_scatter(partial_value, 'rep', scatter_dimension=0, tiled=True)  24.1 us
  transfers between devices with their start and end apart: 3, of which 3 were waited for; matrix products, arithmetic and copies ran while one was open for 1% of the time, Pallas kernels for 0%

commit v1 on v0

--- a/solution.py
+++ b/solution.py
@@ -37,7 +37,15 @@
     own_rows = lax.dynamic_slice_in_dim(tile_row[0], rep_index, 1, 0)
     own_cols = lax.dynamic_slice_in_dim(tile_col[0], rep_index, 1, 0)
     own_count = lax.dynamic_slice_in_dim(tile_count[0], rep_index, 1, 0)
-    stripe_nodes = lax.all_gather(features, "rows", axis=0, tiled=True)
+    stripe_nodes = jnp.concatenate(
+        lax.all_to_all(
+            jnp.stack([features for _ in range(lax.axis_size("rows"))]),
+            axis_name="rows",
+            split_axis=0,
+            concat_axis=0,
+        ),
+        axis=0,
+    )
     blocks = stripe_nodes.reshape(-1, block_size, feature_width)
     partial_value = propagate(
         own_tiles, own_rows, own_cols, own_count, blocks, row_count, slots_wide

time: 483 us -> 563 us (1.17)
  waiting for transfers between devices: 357 us -> 413 us
  starting transfers between devices: 0.12 us -> 20 us
    all_to_all x0 -> x1, waiting for transfers between devices: none -> 203 us  [shards(): lax.all_to_all(jnp.stack([features for _ in range(lax.axis_size('rows'))]...]
    all_gather x1 -> x0, waiting for transfers between devices: 155 us -> none  [shards(): stripe_nodes = lax.all_gather(features, 'rows', axis=0, tiled=True)]
    all_to_all x0 -> x1, starting transfers between devices: none -> 19.9 us  [shards(): lax.all_to_all(jnp.stack([features for _ in range(lax.axis_size('rows'))]...]
    reduce_scatter x1, waiting for transfers between devices: 24.1 us -> 32.6 us  [shards(): lax.psum_scatter(partial_value, 'rep', scatter_dimension=0, tiled=True)]
  transfers between devices with their start and end apart: 3 -> 3, of which waited for: 3 -> 3; matrix products, arithmetic and copies ran while one was open for 1% -> 0% of each run, Pallas kernels for 0% -> 0%
where the time goes in v1:
time: 563 us; the launch traced here: 562 us
  waiting for transfers between devices  413 us (73%)
  blocking collectives  97.2 us (17%)
  starting transfers between devices  20 us (4%)
  between operations  14.1 us (3%)
  local copies, waits for them, and re-layouts  13 us (2%)
    all_to_all x1, waiting for transfers between devices, shards(): lax.all_to_all(jnp.stack([features for _ in range(lax.axis_size('rows'))]...  203 us
    psum x1, waiting for transfers between devices, shards(): weight_grad, bias_grad = lax.psum((weight_term, bias_term), ('rows', 'rep'))  177 us
    psum x1, blocking collectives, shards(): weight_grad, bias_grad = lax.psum((weight_term, bias_term), ('rows', 'rep'))  97.2 us
    reduce_scatter x1, waiting for transfers between devices, shards(): lax.psum_scatter(partial_value, 'rep', scatter_dimension=0, tiled=True)  32.6 us
    all_to_all x1, starting transfers between devices, shards(): lax.all_to_all(jnp.stack([features for _ in range(lax.axis_size('rows'))]...  19.9 us
  transfers between devices with their start and end apart: 3, of which 3 were waited for; matrix products, arithmetic and copies ran while one was open for 0% of the time, Pallas kernels for 0%

profile of v1, /device:TPU:23, one launch (start us, length us, event | category | flops | bytes accessed | tf_op | source)
XLA Modules:
  0.0 562.5 jit_solution(6542214025020552814)
XLA Ops:
  7.2 0.0 copy-start
  7.2 5.2 stack.2
  12.4 0.0 copy-start.5
  12.4 0.0 copy-start.3
  12.4 0.0 copy-start.1
  12.4 0.0 copy-start.2
  12.4 0.0 copy-start.4
  12.4 19.9 %all-to-all-start = ((bf16[128,128,256]{2,1,0:T(8,128)(2,1)}), bf16[128,128,256]{2,1,0:T(8,128)(2,1)}, u32[]{:S(2)}, u32[]{:S(2)}) async-start(bf16[128,128,256]{2,1,0:T(8,128)(2,1)} %stack.2), calls=%async_computation | async-start | bytes 16777216 | tf_op jit(solution)/shard_map/all_to_all | solution.py:41
  32.3 0.0 reduce-scatter.2.cloned.1.call-start
  32.4 0.0 copy-done.5
  32.4 0.6 constant_dynamic-slice_fusion.1
  33.0 0.0 copy-done.3
  33.0 0.7 fusion.17
  33.7 0.6 iota_compare_fusion.1
  34.4 203.1 %all-to-all-done = bf16[128,128,256]{2,1,0:T(8,128)(2,1)} async-done(((bf16[128,128,256]{2,1,0:T(8,128)(2,1)}), bf16[128,128,256]{2,1,0:T(8,128)(2,1)}, u32[]{:S(2)}, u32[]{:S(2)}) %all-to-all-start) | async-done | bytes 8388640 | tf_op jit(solution)/shard_map/all_to_all | solution.py:41
  237.5 4.0 gather_fusion
  241.4 0.0 copy-done
  241.5 0.4 fusion.2
  241.8 0.4 fusion
  242.2 0.9 copy.11
  243.1 0.0 reduce-scatter.2.cloned.1.call-update
  243.1 0.0 all-reduce.2.cloned.1.call-start
  243.2 32.6 %reduce-scatter.2.cloned.1.call-done = f32[128,256]{1,0:T(8,128)} async-done(((f32[512,256]{1,0:T(8,128)}), f32[128,256]{1,0:T(8,128)}) %reduce-scatter.2.cloned.1.call-update) | async-done | bytes 131088 | tf_op jit(solution)/shard_map/reduce_scatter | solution.py:54
  275.8 0.0 copy-done.1
  275.8 0.0 copy-done.2
  275.8 0.0 copy-done.4
  275.8 1.8 convert_reduce_fusion
  277.6 1.8 fusion.8
  279.4 0.0 all-reduce.2.cloned.1.call-update
  279.4 97.2 %psum.15 = f32[256]{0:T(256)} all-reduce(f32[256]{0:T(256)S(1)} %get-tuple-element.3), channel_id=1, replica_groups=mesh['rows'=128,'rep'=4] {'rows','rep'}, use_global_device_ids=true, to_apply=%region_3.4 | all-reduce | flops 256 | bytes 2048 | tf_op jit(solution)/shard_map/psum | solution.py:66
  376.6 177.3 %all-reduce.2.cloned.1.call-done = f32[256,256]{1,0:T(8,128)} async-done(((f32[256,256]{1,0:T(8,128)}), f32[256,256]{1,0:T(8,128)}) %all-reduce.2.cloned.1.call-update) | async-done | bytes 262160 | tf_op jit(solution)/shard_map/psum | solution.py:66
  554.0 1.7 copy.16
  (3 shorter events, 0.0 us)
Async XLA Ops:
  7.2 234.3 %copy-start = (bf16[1,4,8,128,128]{4,3,2,1,0:T(8,128)(2,1)S(1)}, bf16[1,4,8,128,128]{4,3,2,1,0:T(8,128)(2,1)}, u32[]{:S(2)}) copy-start(bf16[1,4,8,128,128]{4,3,2,1,0:T(8,128)(2,1)} %param.11) | copy-start | bytes 3145732
  12.4 20.0 %copy-start.5 = (s32[1,4]{1,0:T(1,128)S(1)}, s32[1,4]{1,0:T(1,128)}, u32[]{:S(2)}) copy-start(s32[1,4]{1,0:T(1,128)} %param.14) | copy-start | bytes 52
  12.4 20.6 %copy-start.3 = (s32[1,4,8]{2,1,0:T(4,128)S(1)}, s32[1,4,8]{2,1,0:T(4,128)}, u32[]{:S(2)}) copy-start(s32[1,4,8]{2,1,0:T(4,128)} %param.13) | copy-start | bytes 388
  12.4 263.4 %copy-start.1 = (bf16[256,256]{1,0:T(8,128)(2,1)S(1)}, bf16[256,256]{1,0:T(8,128)(2,1)}, u32[]{:S(2)}) copy-start(bf16[256,256]{1,0:T(8,128)(2,1)} %param.9) | copy-start | bytes 393220
  12.4 263.4 %copy-start.2 = (bf16[128,256]{1,0:T(8,128)(2,1)S(1)}, bf16[128,256]{1,0:T(8,128)(2,1)}, u32[]{:S(2)}) copy-start(bf16[128,256]{1,0:T(8,128)(2,1)} %param.15) | copy-start | bytes 196612
  12.4 263.4 %copy-start.4 = (f32[256]{0:T(256)S(1)}, f32[256]{0:T(256)}, u32[]{:S(2)}) copy-start(f32[256]{0:T(256)} %param.10) | copy-start | bytes 3076
  12.4 225.1 %all-to-all-start = ((bf16[128,128,256]{2,1,0:T(8,128)(2,1)}), bf16[128,128,256]{2,1,0:T(8,128)(2,1)}, u32[]{:S(2)}, u32[]{:S(2)}) async-start(bf16[128,128,256]{2,1,0:T(8,128)(2,1)} %stack.2), calls=%async_computation | async-start | bytes 16777216 | tf_op jit(solution)/shard_map/all_to_all | solution.py:41
  32.3 243.5 %reduce-scatter.2.cloned.1.call-start = ((), (), s32[]{:S(2)}) async-start(), calls=%async_computation.2 | async-start | bytes 655360 | tf_op jit(solution)/shard_map/reduce_scatter | solution.py:54
  243.1 310.8 %all-reduce.2.cloned.1.call-start = ((), (), s32[]{:S(2)}) async-start(), calls=%async_computation.3 | async-start | bytes 524288 | tf_op jit(solution)/shard_map/psum | solution.py:66
Sparse Core Ops, SparseCore 0:
  243.3 32.4 reduce-scatter.1
  281.3 272.5 all-reduce.1
